TPU v7x, 256 devices: a whole 4x4x8 slice. The times are simulated.
256 devices in a mesh: dp: 32 (over x, y, core), tensor: 8 (over z).
Axes of the slice: x: 4, y: 4, z: 8, core: 2. Of those that a mesh axis runs over, the one named last changes fastest.
Arguments:
- hidden_states: bfloat16 [24576, 4096], P('dp', 'tensor')
- neighbour_ids: int32 [384, 2], P('dp'), may hold values from 0 to 511, as said below
- database: bfloat16 [512, 128, 896], P('dp')
- w_up: bfloat16 [896, 3584], P(None, 'tensor'), may hold values from -0.1875 to 0.1875
- w_down: bfloat16 [3584, 896], P('tensor'), may hold values from -0.09375 to 0.09375
- w_query: bfloat16 [4096, 4096], P(None, 'tensor'), may hold values from -0.09375 to 0.09375
- w_key: bfloat16 [896, 4096], P(None, 'tensor'), may hold values from -0.1875 to 0.1875
- w_value: bfloat16 [896, 4096], P(None, 'tensor'), may hold values from -0.1875 to 0.1875
Outputs:
- attended: bfloat16 [24576, 4096], P('dp', 'tensor')
Inputs may be any that keep to these rules, and one draw needn't show every extreme that they name: `neighbour_ids`: block ids are grouped by owner: index s of dp holds blocks s * 16 to (s + 1) * 16 - 1. Among the 24 ids of one sequence, no owner's blocks are named more than 2 times; one owner, the same for every sequence, is named exactly 2 times by each.
All inputs are finite; a program needn't handle non-finite values.
Results may differ from a plain program's by a relative error of at most 0.02.
Values may be sent and summed in bfloat16 or wider, within the bound.
No kernel may reach another device: no remote copies, remote signals or barrier semaphores. Data moves between devices by JAX's collectives and lax.ppermute only.
A program may use at most 128 MiB of HBM per device.

v0:
```python
import math
import jax
import jax.numpy as jnp
from jax import lax
from jax.sharding import PartitionSpec as P

HD = 128
SPAN = 64
KN = 2
NTOK = 128
EPSILON = 1e-06
LOGIT_SCALE = 3.0


def head_norm(projected):
    shaped = projected.reshape(projected.shape[0], -1, HD)
    scaled = shaped * lax.rsqrt(jnp.mean(shaped * shaped, axis=-1, keepdims=True) + EPSILON)
    return scaled.astype(jnp.bfloat16)


def attend(windows_flat, keys, values):
    heads_here = windows_flat.shape[1]
    span_count = windows_flat.shape[0] // SPAN
    windows = windows_flat.reshape(span_count, SPAN, heads_here, HD)
    key_blocks = keys.reshape(span_count, KN * NTOK, heads_here, HD)
    value_blocks = values.reshape(span_count, KN * NTOK, heads_here, HD)
    scores = jnp.einsum("cqhd,ckhd->chqk", windows, key_blocks, preferred_element_type=jnp.float32)
    scores = scores * (LOGIT_SCALE / math.sqrt(HD))
    expo = jnp.exp(scores)
    weights = (expo / jnp.sum(expo, axis=-1, keepdims=True)).astype(jnp.bfloat16)
    mixed = jnp.einsum("chqk,ckhd->cqhd", weights, value_blocks, preferred_element_type=jnp.float32)
    return mixed.astype(jnp.bfloat16).reshape(span_count * SPAN, heads_here * HD)


def ring_hops(states, n):
    to_right = [(i, (i + 1) % n) for i in range(n)]
    to_left = [(i, (i - 1) % n) for i in range(n)]
    going_right = states
    going_left = states
    right_hops = n // 2
    left_hops = n - 1 - right_hops
    steps = []
    for hop in range(1, right_hops + 1):
        step = {}
        going_right = lax.ppermute(going_right, "tensor", to_right)
        step[(n - hop) % n] = going_right
        if hop <= left_hops:
            going_left = lax.ppermute(going_left, "tensor", to_left)
            step[hop] = going_left
        steps.append(step)
    return steps


def ring_query(got, w_query, n):
    width = got[0].shape[1]
    me = lax.axis_index("tensor")
    total = None
    for offset in range(n):
        rows = lax.dynamic_slice_in_dim(w_query, (me + offset) % n * width, width, 0)
        term = jnp.dot(got[offset], rows, preferred_element_type=jnp.float32)
        total = term if total is None else total + term
    return total


def shards(hidden_states, neighbour_ids, database, w_up, w_down, w_query, w_key, w_value):
    dp_count = lax.axis_size("dp")
    tensor_count = lax.axis_size("tensor")
    shard_blocks = database.shape[0]
    block_tokens = database.shape[1]
    enc_width = database.shape[2]
    flat_ids = neighbour_ids.reshape(-1)
    request_count = flat_ids.shape[0]
    capacity = max(2, (request_count + dp_count - 1) // dp_count + 1)
    owners = flat_ids // shard_blocks
    local_rows = flat_ids % shard_blocks
    owner_match = (owners[:, None] == jnp.arange(dp_count, dtype=jnp.int32)[None, :]).astype(
        jnp.int32
    )
    positions = jnp.arange(request_count, dtype=jnp.int32)
    earlier = (positions[:, None] > positions[None, :]).astype(jnp.int32)
    ranks = jnp.sum(jnp.dot(earlier, owner_match) * owner_match, axis=1)
    slots = owners * capacity + ranks
    slot_match = slots[None, :] == jnp.arange(dp_count * capacity, dtype=jnp.int32)[:, None]
    requests = jnp.sum(jnp.where(slot_match, local_rows[None, :], 0), axis=1)
    requests = requests.reshape(dp_count, capacity)
    pieces = dp_count
    me_dp = lax.axis_index("dp")
    up_piece = lax.dynamic_slice_in_dim(
        w_up, me_dp * (w_up.shape[0] // pieces), w_up.shape[0] // pieces, 0
    )
    down_piece = lax.dynamic_slice_in_dim(
        w_down, me_dp * (w_down.shape[0] // pieces), w_down.shape[0] // pieces, 0
    )
    up_all = lax.all_gather(lax.all_gather(up_piece, "tensor"), "dp")
    down_all = lax.all_gather(lax.all_gather(down_piece, "tensor"), "dp")
    rows_here = block_tokens // tensor_count
    raw_float = database.astype(jnp.float32)
    raw_own = lax.dynamic_slice_in_dim(
        raw_float, lax.axis_index("tensor") * rows_here, rows_here, 1
    )
    normed = (
        raw_own * lax.rsqrt(jnp.mean(raw_own * raw_own, axis=-1, keepdims=True) + EPSILON)
    ).astype(jnp.bfloat16)
    states = hidden_states[SPAN - 1 :]
    steps = ring_hops(states, tensor_count)
    got = {0: states}
    for step in steps:
        got.update(step)
    early = [v for step in steps[: len(steps) // 2] for v in step.values()]
    late = [v for step in steps[len(steps) // 2 :] for v in step.values()]
    normed, _ = lax.optimization_barrier((normed, early))
    flat_normed = normed.reshape(shard_blocks * rows_here, pieces, enc_width // pieces)
    inner = jnp.einsum("ncr,cgrh->ngh", flat_normed, up_all, preferred_element_type=jnp.float32)
    active = jax.nn.gelu(inner).astype(jnp.bfloat16)
    active = active.reshape(active.shape[0], tensor_count, pieces, -1)
    partials = jnp.einsum("ngcr,cgre->gne", active, down_all, preferred_element_type=jnp.float32)
    summed = jnp.sum(partials.astype(jnp.bfloat16).astype(jnp.float32), axis=0)
    summed = summed.reshape(shard_blocks, rows_here, enc_width)
    encoded_own = (raw_own + summed).astype(jnp.bfloat16)
    asked = lax.all_to_all(requests, "dp", split_axis=0, concat_axis=0, tiled=True)
    served, _ = lax.optimization_barrier((encoded_own[asked], late))
    replies = lax.all_to_all(served, "dp", split_axis=0, concat_axis=0, tiled=True)
    mine = replies.reshape(dp_count * capacity, rows_here, enc_width)[slots]
    queries = head_norm(ring_query(got, w_query, tensor_count))
    padded = jnp.concatenate(
        [queries, jnp.zeros((SPAN - 1,) + queries.shape[1:], queries.dtype)], axis=0
    )
    encoded = lax.all_gather(mine, "tensor", axis=1, tiled=True)
    flat_encoded = encoded.reshape(-1, enc_width)
    keys = head_norm(jnp.dot(flat_encoded, w_key, preferred_element_type=jnp.float32))
    values = jnp.dot(flat_encoded, w_value, preferred_element_type=jnp.float32).astype(jnp.bfloat16)
    values = values.reshape(flat_encoded.shape[0], -1, HD)
    mixed = [attend(padded, keys, values)]
    mixed = jnp.concatenate(mixed, axis=0)
    heads_width = mixed.shape[1]
    leading = jnp.zeros((SPAN - 1, heads_width), jnp.bfloat16)
    return jnp.concatenate([leading, mixed[: mixed.shape[0] - SPAN + 1]], axis=0)


def solution(mesh):
    in_specs = (
        P("dp", "tensor"),
        P("dp", None),
        P("dp", None, None),
        P(None, "tensor"),
        P("tensor", None),
        P(None, "tensor"),
        P(None, "tensor"),
        P(None, "tensor"),
    )
    out_specs = P("dp", "tensor")
    return jax.shard_map(shards, mesh=mesh, in_specs=in_specs, out_specs=out_specs, check_vma=False)
```

profile of v0, /device:TPU:1, one launch (start us, length us, event | category | flops | bytes accessed | tf_op | source)
XLA Modules:
  0.0 297.0 jit_solution(3649769576130073630)
XLA Ops:
  6.5 1.1 constant_dynamic-slice_fusion
  7.7 0.1 copy.115
  7.8 23.3 %all-gather.5 = bf16[8,28,448]{2,1,0:T(8,128)(2,1)S(1)} all-gather(bf16[1,28,448]{2,1,0:T(8,128)(2,1)S(1)} %bitcast.67), channel_id=2, replica_groups=mesh['dp'=32,'tensor'=8] {'tensor'}, dimensions={0}, use_global_device_ids=true | all-gather | bytes 225792 | tf_op jit(solution)/shard_map/all_gather | solution.py:94
  31.1 0.8 copy.93
  32.0 0.8 dynamic-slice_bitcast_fusion
  32.8 18.7 %all-gather.6 = bf16[8,14,896]{2,1,0:T(8,128)(2,1)S(1)} all-gather(bf16[1,14,896]{2,1,0:T(8,128)(2,1)S(1)} %dynamic-slice_bitcast_fusion), channel_id=4, replica_groups=mesh['dp'=32,'tensor'=8] {'tensor'}, dimensions={0}, use_global_device_ids=true | all-gather | bytes 225792 | tf_op jit(solution)/shard_map/all_gather | solution.py:95
  51.5 0.7 copy.97
  52.2 1.3 slice.6
  53.5 0.7 collective-permute-start
  54.2 2.1 collective-permute-start.1
  56.3 9.1 %collective-permute-done = bf16[705,512]{1,0:T(8,128)(2,1)S(1)} collective-permute-done((bf16[705,512]{1,0:T(8,128)(2,1)S(1)}, bf16[705,512]{1,0:T(8,128)(2,1)S(1)}, u32[]{:S(2)}, u32[]{:S(2)}) %collective-permute-start) | collective-permute-done | bytes 721952 | tf_op jit(solution)/shard_map/ppermute | solution.py:45
  65.4 0.1 copy.100
  65.5 0.1 reshape.245
  65.6 0.3 fusion.35
  65.9 0.1 select_reduce_fusion
  66.0 0.7 all_to_all.11
  66.7 27.0 %all-to-all-start = ((s32[32,1,2]{2,1,0:T(1,128)}), s32[32,1,2]{2,1,0:T(1,128)S(1)}, u32[]{:S(2)}, u32[]{:S(2)}) async-start(s32[32,1,2]{2,1,0:T(1,128)} %bitcast.11), calls=%async_computation | async-start | bytes 32768 | tf_op jit(solution)/shard_map/all_to_all | solution.py:120
  93.8 1.2 fusion.37
  95.0 3.0 %collective-permute-start.3 = (bf16[705,512]{1,0:T(8,128)(2,1)S(1)}, bf16[705,512]{1,0:T(8,128)(2,1)}, u32[]{:S(2)}, u32[]{:S(2)}) collective-permute-start(bf16[705,512]{1,0:T(8,128)(2,1)S(1)} %collective-permute-done.1), channel_id=1, source_target_pairs={{0,7},{1,0},{2,1},{3,2},{4,3},{5,4},{6,5},{7,6},{8,15},{9,8},{10,9... | collective-permute-start | bytes 2165768 | tf_op jit(solution)/shard_map/ppermute | solution.py:48
  98.0 1.2 fusion.38
  99.2 1.5 all-to-all-done
  100.7 0.1 copy.102
  100.8 0.1 copy.103
  100.9 0.1 reshape.255
  101.0 12.4 %collective-permute-done.3 = bf16[705,512]{1,0:T(8,128)(2,1)} collective-permute-done((bf16[705,512]{1,0:T(8,128)(2,1)S(1)}, bf16[705,512]{1,0:T(8,128)(2,1)}, u32[]{:S(2)}, u32[]{:S(2)}) %collective-permute-start.3) | collective-permute-done | bytes 721952 | tf_op jit(solution)/shard_map/ppermute | solution.py:48
  113.4 5.3 %reshape.242 = bf16[256,32,28]{2,1,0:T(8,128)(2,1)S(1)} reshape(bf16[16,16,896]{2,1,0:T(8,128)(2,1)S(1)} %fusion.38) | data formatting | bytes 917504 | tf_op jit(solution)/shard_map/reshape | solution.py:112
  118.8 3.0 %copy.94 = bf16[256,32,28]{0,1,2:T(8,128)(2,1)} copy(bf16[256,32,28]{2,1,0:T(8,128)(2,1)S(1)} %reshape.242) | data formatting | bytes 917504 | tf_op jit(solution)/shard_map/reshape | solution.py:112
  121.8 3.5 %collective-permute-start.5 = (bf16[705,512]{1,0:T(8,128)(2,1)}, bf16[705,512]{1,0:T(8,128)(2,1)}, u32[]{:S(2)}, u32[]{:S(2)}) collective-permute-start(bf16[705,512]{1,0:T(8,128)(2,1)} %collective-permute-done.3), channel_id=1, source_target_pairs={{0,7},{1,0},{2,1},{3,2},{4,3},{5,4},{6,5},{7,6},{8,15},{9,8},{10,9... | collective-permute-start | bytes 2165768 | tf_op jit(solution)/shard_map/ppermute | solution.py:48
  125.3 8.6 %fusion.11 = bf16[256,8,448]{0,2,1:T(8,128)(2,1)S(1)} fusion(bf16[32,8,28,448]{3,1,0,2:T(8,128)(2,1)} %bitcast.68, bf16[256,32,28]{0,1,2:T(8,128)(2,1)} %copy.94), kind=kOutput, calls=%fused_computation.19 | convolution fusion | flops 1652424704 | bytes 8716288 | tf_op jit(solution)/shard_map/ncr,cgrh->ngh/dot_general | solution.py:113
  133.9 1.0 copy.96
  134.9 20.9 %all-gather.13.cloned.1.call-done = bf16[256,14,896]{2,0,1:T(8,128)(2,1)} async-done(((bf16[8,14,896]{2,0,1:T(8,128)(2,1)}), bf16[256,14,896]{2,0,1:T(8,128)(2,1)}) %all-gather.13.cloned.1.call-update) | async-done | bytes 6422544 | tf_op jit(solution)/shard_map/all_gather | solution.py:95
  155.8 6.7 %convert_reduce_fusion = f32[256,896]{1,0:T(8,128)S(1)} fusion(bf16[32,8,14,896]{3,1,0,2:T(8,128)(2,1)} %bitcast.69, bf16[256,8,32,14]{0,1,3,2:T(8,128)(2,1)S(1)} %bitcast.63), kind=kOutput, calls=%fused_computation.5 | convolution fusion | flops 1649442816 | bytes 9175040 | tf_op jit(solution)/shard_map/ngcr,cgre->gne/dot_general | solution.py:116
  162.5 1.1 fusion.36
  163.6 2.0 gather_fusion
  165.6 4.7 %all-to-all-start.1 = ((bf16[32,2,16,896]{3,2,1,0:T(8,128)(2,1)}), bf16[32,2,16,896]{3,2,1,0:T(8,128)(2,1)S(1)}, u32[]{:S(2)}, u32[]{:S(2)}) async-start(bf16[32,2,16,896]{3,2,1,0:T(8,128)(2,1)} %bitcast.13), calls=%async_computation.1 | async-start | bytes 3670016 | tf_op jit(solution)/shard_map/all_to_all | solution.py:122
  170.3 0.3 all-gather.15.cloned.1.call-start
  170.6 0.1 reshape.247
  170.7 25.1 %all-to-all-done.1 = bf16[32,2,16,896]{3,2,1,0:T(8,128)(2,1)S(1)} async-done(((bf16[32,2,16,896]{3,2,1,0:T(8,128)(2,1)}), bf16[32,2,16,896]{3,2,1,0:T(8,128)(2,1)S(1)}, u32[]{:S(2)}, u32[]{:S(2)}) %all-to-all-start.1) | async-done | bytes 1835040 | tf_op jit(solution)/shard_map/all_to_all | solution.py:122
  195.8 1.5 gather_fusion.1
  197.5 2.3 copy.114
  199.8 2.0 fusion.50
  201.8 0.6 copy-done.1
  202.4 0.5 fusion.40
  202.9 0.6 convolution_add_fusion.3
  203.5 1.7 fusion.42
  205.2 1.7 convolution_add_fusion.2
  206.8 1.7 fusion.44
  208.5 1.7 convolution_add_fusion.1
  210.2 1.8 fusion.27
  211.9 1.8 reshape.249
  213.7 0.8 multiply_reduce_fusion.1
  214.5 0.1 copy.105
  214.7 0.4 fusion.28
  215.2 46.8 %all-gather.15.cloned.1.call-done = bf16[24,128,896]{2,1,0:T(8,128)(2,1)} async-done(((bf16[24,16,896]{2,1,0:T(8,128)(2,1)}), bf16[24,128,896]{2,1,0:T(8,128)(2,1)}) %all-gather.15.cloned.1.call-update) | async-done | bytes 5505040 | tf_op jit(solution)/shard_map/all_gather | solution.py:128
  262.0 8.7 %multiply_reduce_fusion = (f32[3072,4]{0,1:T(4,128)S(1)}, f32[3072,4,128]{2,0,1:T(8,128)}) fusion(bf16[3072,896,1]{1,0,2:T(8,128)(2,1)} %bitcast.70, bf16[4,128,896]{2,1,0:T(8,128)(2,1)S(1)} %bitcast.65), kind=kOutput, calls=%fused_computation.9 | convolution fusion | flops 2821705728 | bytes 12763136 | tf_op jit(solution)/shard_map/dot_general | solution.py:130
  270.8 4.8 %convolution_convert_fusion = bf16[3072,512]{1,0:T(8,128)(2,1)} fusion(bf16[3072,896]{1,0:T(8,128)(2,1)S(1)} %bitcast.71, bf16[896,512]{1,0:T(8,128)(2,1)S(1)} %copy-done), kind=kOutput, calls=%fused_computation.11 | convolution fusion | flops 2820145152 | bytes 9568256 | tf_op jit(solution)/shard_map/dot_general | solution.py:131
  275.5 5.5 %reshape_reshape.3 = bf16[12,256,4,128]{3,2,1,0:T(4,128)(2,1)} reshape(bf16[3072,512]{1,0:T(8,128)(2,1)} %convolution_convert_fusion) | data formatting | bytes 6291456 | tf_op jit(solution)/shard_map/reshape;reshape | solution.py:26
  281.1 4.4 %multiply_convert_fusion = bf16[3072,4,128]{2,0,1:T(8,128)(2,1)S(1)} fusion(f32[3072,4,128]{2,0,1:T(8,128)} %get-tuple-element.12, f32[3072,4]{0,1:T(4,128)S(1)} %add_rsqrt_fusion), kind=kLoop, calls=%fused_computation.8 | loop fusion | flops 3145728 | bytes 9486336 | tf_op jit(solution)/shard_map/convert_element_type | solution.py:18
  285.5 1.3 fusion.16
  286.8 0.6 copy-done.2
  287.4 1.2 fusion.32
  288.6 0.6 copy.111
  289.2 0.1 copy.145
  289.4 1.1 concatenate.7
  (43 shorter events, 0.4 us)
Async XLA Ops:
  6.5 264.2 %copy-start = (bf16[896,512]{1,0:T(8,128)(2,1)S(1)}, bf16[896,512]{1,0:T(8,128)(2,1)}, u32[]{:S(2)}) copy-start(bf16[896,512]{1,0:T(8,128)(2,1)} %param.15) | copy-start | bytes 2752516
  6.5 58.9 %copy-start.8 = (s32[12,2]{0,1:T(2,128)S(1)}, s32[12,2]{0,1:T(2,128)}, u32[]{:S(2)}) copy-start(s32[12,2]{0,1:T(2,128)} %param.9) | copy-start | bytes 292
  6.5 118.8 %all-gather.11.cloned.1.call-start = ((), (), s32[]{:S(2)}) async-start(), calls=%async_computation.2 | async-start | bytes 7569408 | tf_op jit(solution)/shard_map/all_gather | solution.py:94
  31.9 123.9 %all-gather.13.cloned.1.call-start = ((), (), s32[]{:S(2)}) async-start(), calls=%async_computation.3 | async-start | bytes 6623232 | tf_op jit(solution)/shard_map/all_gather | solution.py:95
  53.5 11.9 %collective-permute-start = (bf16[705,512]{1,0:T(8,128)(2,1)S(1)}, bf16[705,512]{1,0:T(8,128)(2,1)S(1)}, u32[]{:S(2)}, u32[]{:S(2)}) collective-permute-start(bf16[705,512]{1,0:T(8,128)(2,1)S(1)} %slice.6), channel_id=1, source_target_pairs={{0,1},{1,2},{2,3},{3,4},{4,5},{5,6},{6,7},{7,0},{8,9},{9,10},{10,1... | collective-permute-start | bytes 2165768 | tf_op jit(solution)/shard_map/ppermute | solution.py:45
  54.2 40.8 %collective-permute-start.1 = (bf16[705,512]{1,0:T(8,128)(2,1)S(1)}, bf16[705,512]{1,0:T(8,128)(2,1)S(1)}, u32[]{:S(2)}, u32[]{:S(2)}) collective-permute-start(bf16[705,512]{1,0:T(8,128)(2,1)S(1)} %slice.6), channel_id=1, source_target_pairs={{0,7},{1,0},{2,1},{3,2},{4,3},{5,4},{6,5},{7,6},{8,15},{9,8},{10,9... | collective-permute-start | bytes 2165768 | tf_op jit(solution)/shard_map/ppermute | solution.py:48
  65.4 35.6 %copy-start.4 = (bf16[705,512]{1,0:T(8,128)(2,1)}, bf16[705,512]{1,0:T(8,128)(2,1)S(1)}, u32[]{:S(2)}) copy-start(bf16[705,512]{1,0:T(8,128)(2,1)S(1)} %collective-permute-done) | copy-start | bytes 2165764
  65.4 32.6 %collective-permute-start.2 = (bf16[705,512]{1,0:T(8,128)(2,1)S(1)}, bf16[705,512]{1,0:T(8,128)(2,1)}, u32[]{:S(2)}, u32[]{:S(2)}) collective-permute-start(bf16[705,512]{1,0:T(8,128)(2,1)S(1)} %collective-permute-done), channel_id=1, source_target_pairs={{0,1},{1,2},{2,3},{3,4},{4,5},{5,6},{6,7},{7,0},{8,9},{9,10},{10,1... | collective-permute-start | bytes 2165768 | tf_op jit(solution)/shard_map/ppermute | solution.py:45
  66.7 34.0 %all-to-all-start = ((s32[32,1,2]{2,1,0:T(1,128)}), s32[32,1,2]{2,1,0:T(1,128)S(1)}, u32[]{:S(2)}, u32[]{:S(2)}) async-start(s32[32,1,2]{2,1,0:T(1,128)} %bitcast.11), calls=%async_computation | async-start | bytes 32768 | tf_op jit(solution)/shard_map/all_to_all | solution.py:120
  95.0 6.1 %copy-start.6 = (bf16[705,512]{1,0:T(8,128)(2,1)}, bf16[705,512]{1,0:T(8,128)(2,1)S(1)}, u32[]{:S(2)}) copy-start(bf16[705,512]{1,0:T(8,128)(2,1)S(1)} %collective-permute-done.1) | copy-start | bytes 2165764
  95.0 18.5 %collective-permute-start.3 = (bf16[705,512]{1,0:T(8,128)(2,1)S(1)}, bf16[705,512]{1,0:T(8,128)(2,1)}, u32[]{:S(2)}, u32[]{:S(2)}) collective-permute-start(bf16[705,512]{1,0:T(8,128)(2,1)S(1)} %collective-permute-done.1), channel_id=1, source_target_pairs={{0,7},{1,0},{2,1},{3,2},{4,3},{5,4},{6,5},{7,6},{8,15},{9,8},{10,9... | collective-permute-start | bytes 2165768 | tf_op jit(solution)/shard_map/ppermute | solution.py:48
  98.0 27.3 %collective-permute-start.4 = (bf16[705,512]{1,0:T(8,128)(2,1)}, bf16[705,512]{1,0:T(8,128)(2,1)}, u32[]{:S(2)}, u32[]{:S(2)}) collective-permute-start(bf16[705,512]{1,0:T(8,128)(2,1)} %collective-permute-done.2), channel_id=1, source_target_pairs={{0,1},{1,2},{2,3},{3,4},{4,5},{5,6},{6,7},{7,0},{8,9},{9,10},{10,1... | collective-permute-start | bytes 2165768 | tf_op jit(solution)/shard_map/ppermute | solution.py:45
  121.8 43.9 %collective-permute-start.5 = (bf16[705,512]{1,0:T(8,128)(2,1)}, bf16[705,512]{1,0:T(8,128)(2,1)}, u32[]{:S(2)}, u32[]{:S(2)}) collective-permute-start(bf16[705,512]{1,0:T(8,128)(2,1)} %collective-permute-done.3), channel_id=1, source_target_pairs={{0,7},{1,0},{2,1},{3,2},{4,3},{5,4},{6,5},{7,6},{8,15},{9,8},{10,9... | collective-permute-start | bytes 2165768 | tf_op jit(solution)/shard_map/ppermute | solution.py:48
  125.3 40.3 %collective-permute-start.6 = (bf16[705,512]{1,0:T(8,128)(2,1)}, bf16[705,512]{1,0:T(8,128)(2,1)S(1)}, u32[]{:S(2)}, u32[]{:S(2)}) collective-permute-start(bf16[705,512]{1,0:T(8,128)(2,1)} %collective-permute-done.4), channel_id=1, source_target_pairs={{0,1},{1,2},{2,3},{3,4},{4,5},{5,6},{6,7},{7,0},{8,9},{9,10},{10,1... | collective-permute-start | bytes 2165768 | tf_op jit(solution)/shard_map/ppermute | solution.py:45
  165.6 30.2 %all-to-all-start.1 = ((bf16[32,2,16,896]{3,2,1,0:T(8,128)(2,1)}), bf16[32,2,16,896]{3,2,1,0:T(8,128)(2,1)S(1)}, u32[]{:S(2)}, u32[]{:S(2)}) async-start(bf16[32,2,16,896]{3,2,1,0:T(8,128)(2,1)} %bitcast.13), calls=%async_computation.1 | async-start | bytes 3670016 | tf_op jit(solution)/shard_map/all_to_all | solution.py:122
  170.3 91.7 %all-gather.15.cloned.1.call-start = ((), (), s32[]{:S(2)}) async-start(), calls=%async_computation.4 | async-start | bytes 6193152 | tf_op jit(solution)/shard_map/all_gather | solution.py:128
  197.5 4.3 %copy-start.5 = (bf16[705,512]{1,0:T(8,128)(2,1)S(1)}, bf16[705,512]{1,0:T(8,128)(2,1)}, u32[]{:S(2)}) copy-start(bf16[705,512]{1,0:T(8,128)(2,1)} %copy-done.4) | copy-start | bytes 2165764
  199.8 2.6 copy-start.1
  199.8 3.1 %copy-start.7 = (bf16[705,512]{1,0:T(8,128)(2,1)S(1)}, bf16[705,512]{1,0:T(8,128)(2,1)}, u32[]{:S(2)}) copy-start(bf16[705,512]{1,0:T(8,128)(2,1)} %copy-done.6) | copy-start | bytes 2165764
  214.6 47.4 %copy-start.3 = (bf16[512,896]{1,0:T(8,128)(2,1)S(1)}, bf16[512,896]{1,0:T(8,128)(2,1)}, u32[]{:S(2)}) copy-start(bf16[512,896]{1,0:T(8,128)(2,1)} %copy.114) | copy-start | bytes 2752516
  262.0 8.7 %copy-start.9 = (bf16[24,128,896]{2,1,0:T(8,128)(2,1)S(1)}, bf16[24,128,896]{2,1,0:T(8,128)(2,1)}, u32[]{:S(2)}) copy-start(bf16[24,128,896]{2,1,0:T(8,128)(2,1)} %all-gather.15.cloned.1.call-done) | copy-start | bytes 16515076
  285.5 1.9 copy-start.2
Sparse Core Ops, SparseCore 0:
  32.0 66.9 all-gather.10
  101.6 54.1 all-gather.12
  197.5 64.4 all-gather.14
where the time goes:
time: 298 us; the launch traced here: 297 us
  waiting for transfers between devices  116 us (39%)
  matrix products  43 us (14%)
  blocking collectives  42 us (14%)
  starting transfers between devices  41.3 us (14%)
  local copies, waits for them, and re-layouts  31.8 us (11%)
  between operations  13.6 us (5%)
  other arithmetic  9.35 us (3%)
    all_gather x1, waiting for transfers between devices, shards(): encoded = lax.all_gather(mine, 'tensor', axis=1, tiled=True)  46.8 us
    all_to_all x1, starting transfers between devices, shards(): lax.all_to_all(requests, 'dp', split_axis=0, concat_axis=0, tiled=True)  27 us
    all_to_all x1, waiting for transfers between devices, shards(): lax.all_to_all(served, 'dp', split_axis=0, concat_axis=0, tiled=True)  25.1 us
    all_gather x1, blocking collectives, shards(): up_all = lax.all_gather(lax.all_gather(up_piece, 'tensor'), 'dp')  23.3 us
    all_gather x1, waiting for transfers between devices, shards(): down_all = lax.all_gather(lax.all_gather(down_piece, 'tensor'), 'dp')  20.9 us
    all_gather x1, blocking collectives, shards(): down_all = lax.all_gather(lax.all_gather(down_piece, 'tensor'), 'dp')  18.7 us
    ppermute x3, waiting for transfers between devices, ring_hops(): going_left = lax.ppermute(going_left, 'tensor', to_left)  12.4 us
    dot_general x8, matrix products, ring_query(): term = jnp.dot(got[offset], rows, preferred_element_type=jnp.float32)  11.5 us
  transfers between devices with their start and end apart: 12, of which 6 were waited for; matrix products, arithmetic and copies ran while one was open for 17% of the time, Pallas kernels for 0%

commit v1 on v0

--- a/solution.py
+++ b/solution.py
@@ -125,7 +125,9 @@
     padded = jnp.concatenate(
         [queries, jnp.zeros((SPAN - 1,) + queries.shape[1:], queries.dtype)], axis=0
     )
-    encoded = lax.all_gather(mine, "tensor", axis=1, tiled=True)
+    encoded = jnp.concatenate(
+        lax.all_to_all(jnp.stack([mine] * lax.axis_size("tensor")), "tensor", 0, 0), axis=1
+    )
     flat_encoded = encoded.reshape(-1, enc_width)
     keys = head_norm(jnp.dot(flat_encoded, w_key, preferred_element_type=jnp.float32))
     values = jnp.dot(flat_encoded, w_value, preferred_element_type=jnp.float32).astype(jnp.bfloat16)

time: 298 us -> 368 us (1.23)
  waiting for transfers between devices: 116 us -> 178 us
  starting transfers between devices: 41.3 us -> 47.9 us
  local copies, waits for them, and re-layouts: 31.8 us -> 36.3 us
    all_to_all x0 -> x1, waiting for transfers between devices: none -> 108 us  [shards(): lax.all_to_all(jnp.stack([mine] * lax.axis_size('tensor')), 'tensor', 0, 0)]
    all_gather x1 -> x0, waiting for transfers between devices: 46.8 us -> none  [shards(): encoded = lax.all_gather(mine, 'tensor', axis=1, tiled=True)]
    all_to_all x0 -> x1, starting transfers between devices: none -> 6.87 us  [shards(): lax.all_to_all(jnp.stack([mine] * lax.axis_size('tensor')), 'tensor', 0, 0)]
  transfers between devices with their start and end apart: 12 -> 12, of which waited for: 6 -> 6; matrix products, arithmetic and copies ran while one was open for 17% -> 14% of each run, Pallas kernels for 0% -> 0%
where the time goes in v1:
time: 368 us; the launch traced here: 367 us
  waiting for transfers between devices  178 us (48%)
  starting transfers between devices  47.9 us (13%)
  blocking collectives  42 us (11%)
  matrix products  39.8 us (11%)
  local copies, waits for them, and re-layouts  36.3 us (10%)
  between operations  13.8 us (4%)
  other arithmetic  9.36 us (3%)
    all_to_all x1, waiting for transfers between devices, shards(): lax.all_to_all(jnp.stack([mine] * lax.axis_size('tensor')), 'tensor', 0, 0)  108 us
    all_to_all x1, starting transfers between devices, shards(): lax.all_to_all(requests, 'dp', split_axis=0, concat_axis=0, tiled=True)  27 us
    all_to_all x1, waiting for transfers between devices, shards(): lax.all_to_all(served, 'dp', split_axis=0, concat_axis=0, tiled=True)  25.4 us
    all_gather x1, blocking collectives, shards(): up_all = lax.all_gather(lax.all_gather(up_piece, 'tensor'), 'dp')  23.3 us
    all_gather x1, waiting for transfers between devices, shards(): down_all = lax.all_gather(lax.all_gather(down_piece, 'tensor'), 'dp')  20.9 us
    all_gather x1, blocking collectives, shards(): down_all = lax.all_gather(lax.all_gather(down_piece, 'tensor'), 'dp')  18.7 us
    ppermute x3, waiting for transfers between devices, ring_hops(): going_left = lax.ppermute(going_left, 'tensor', to_left)  12.4 us
    dot_general x8, matrix products, ring_query(): term = jnp.dot(got[offset], rows, preferred_element_type=jnp.float32)  11.3 us
  transfers between devices with their start and end apart: 12, of which 6 were waited for; matrix products, arithmetic and copies ran while one was open for 14% of the time, Pallas kernels for 0%

profile of v1, /device:TPU:1, one launch (start us, length us, event | category | flops | bytes accessed | tf_op | source)
XLA Modules:
  0.0 367.0 jit_solution(7654930567812031334)
XLA Ops:
  6.5 1.1 constant_dynamic-slice_fusion
  7.7 0.1 copy.118
  7.8 23.3 %all-gather.4 = bf16[8,28,448]{2,1,0:T(8,128)(2,1)S(1)} all-gather(bf16[1,28,448]{2,1,0:T(8,128)(2,1)S(1)} %bitcast.70), channel_id=2, replica_groups=mesh['dp'=32,'tensor'=8] {'tensor'}, dimensions={0}, use_global_device_ids=true | all-gather | bytes 225792 | tf_op jit(solution)/shard_map/all_gather | solution.py:94
  31.1 0.8 copy.95
  32.0 0.8 dynamic-slice_bitcast_fusion
  32.8 18.7 %all-gather.5 = bf16[8,14,896]{2,1,0:T(8,128)(2,1)S(1)} all-gather(bf16[1,14,896]{2,1,0:T(8,128)(2,1)S(1)} %dynamic-slice_bitcast_fusion), channel_id=4, replica_groups=mesh['dp'=32,'tensor'=8] {'tensor'}, dimensions={0}, use_global_device_ids=true | all-gather | bytes 225792 | tf_op jit(solution)/shard_map/all_gather | solution.py:95
  51.5 0.7 copy.99
  52.2 1.3 slice.6
  53.5 0.7 collective-permute-start
  54.2 2.1 collective-permute-start.1
  56.3 9.1 %collective-permute-done = bf16[705,512]{1,0:T(8,128)(2,1)S(1)} collective-permute-done((bf16[705,512]{1,0:T(8,128)(2,1)S(1)}, bf16[705,512]{1,0:T(8,128)(2,1)S(1)}, u32[]{:S(2)}, u32[]{:S(2)}) %collective-permute-start) | collective-permute-done | bytes 721952 | tf_op jit(solution)/shard_map/ppermute | solution.py:45
  65.4 0.1 copy.102
  65.5 0.1 reshape.247
  65.6 0.3 fusion.35
  65.9 0.1 select_reduce_fusion
  66.0 0.7 all_to_all.14
  66.7 27.0 %all-to-all-start = ((s32[32,1,2]{2,1,0:T(1,128)}), s32[32,1,2]{2,1,0:T(1,128)S(1)}, u32[]{:S(2)}, u32[]{:S(2)}) async-start(s32[32,1,2]{2,1,0:T(1,128)} %bitcast.11), calls=%async_computation | async-start | bytes 32768 | tf_op jit(solution)/shard_map/all_to_all | solution.py:120
  93.8 1.2 fusion.37
  95.0 3.0 collective-permute-start.3
  98.0 1.2 fusion.38
  99.2 1.5 all-to-all-done
  100.8 0.1 copy.105
  100.9 0.1 reshape.257
  101.0 12.4 %collective-permute-done.3 = bf16[705,512]{1,0:T(8,128)(2,1)} collective-permute-done((bf16[705,512]{1,0:T(8,128)(2,1)S(1)}, bf16[705,512]{1,0:T(8,128)(2,1)}, u32[]{:S(2)}, u32[]{:S(2)}) %collective-permute-start.3) | collective-permute-done | bytes 721952 | tf_op jit(solution)/shard_map/ppermute | solution.py:48
  113.4 5.3 %reshape.244 = bf16[256,32,28]{2,1,0:T(8,128)(2,1)S(1)} reshape(bf16[16,16,896]{2,1,0:T(8,128)(2,1)S(1)} %fusion.38) | data formatting | bytes 917504 | tf_op jit(solution)/shard_map/reshape | solution.py:112
  118.8 3.0 copy.96
  121.7 3.5 collective-permute-start.5
  125.3 8.6 %fusion.11 = bf16[256,8,448]{0,2,1:T(8,128)(2,1)S(1)} fusion(bf16[32,8,28,448]{3,1,0,2:T(8,128)(2,1)} %bitcast.71, bf16[256,32,28]{0,1,2:T(8,128)(2,1)} %copy.96), kind=kOutput, calls=%fused_computation.19 | convolution fusion | flops 1652424704 | bytes 8716288 | tf_op jit(solution)/shard_map/ncr,cgrh->ngh/dot_general | solution.py:113
  133.9 1.0 copy.98
  134.9 20.9 %all-gather.11.cloned.1.call-done = bf16[256,14,896]{2,0,1:T(8,128)(2,1)} async-done(((bf16[8,14,896]{2,0,1:T(8,128)(2,1)}), bf16[256,14,896]{2,0,1:T(8,128)(2,1)}) %all-gather.11.cloned.1.call-update) | async-done | bytes 6422544 | tf_op jit(solution)/shard_map/all_gather | solution.py:95
  155.8 6.7 %convert_reduce_fusion = f32[256,896]{1,0:T(8,128)S(1)} fusion(bf16[32,8,14,896]{3,1,0,2:T(8,128)(2,1)} %bitcast.72, bf16[256,8,32,14]{0,1,3,2:T(8,128)(2,1)S(1)} %bitcast.66), kind=kOutput, calls=%fused_computation.5 | convolution fusion | flops 1649442816 | bytes 9175040 | tf_op jit(solution)/shard_map/ngcr,cgre->gne/dot_general | solution.py:116
  162.5 1.1 fusion.36
  163.6 2.0 gather_fusion
  165.7 4.7 %all-to-all-start.1 = ((bf16[32,2,16,896]{3,2,1,0:T(8,128)(2,1)}), bf16[32,2,16,896]{3,2,1,0:T(8,128)(2,1)S(1)}, u32[]{:S(2)}, u32[]{:S(2)}) async-start(bf16[32,2,16,896]{3,2,1,0:T(8,128)(2,1)} %bitcast.13), calls=%async_computation.1 | async-start | bytes 3670016 | tf_op jit(solution)/shard_map/all_to_all | solution.py:122
  170.5 25.4 %all-to-all-done.1 = bf16[32,2,16,896]{3,2,1,0:T(8,128)(2,1)S(1)} async-done(((bf16[32,2,16,896]{3,2,1,0:T(8,128)(2,1)}), bf16[32,2,16,896]{3,2,1,0:T(8,128)(2,1)S(1)}, u32[]{:S(2)}, u32[]{:S(2)}) %all-to-all-start.1) | async-done | bytes 1835040 | tf_op jit(solution)/shard_map/all_to_all | solution.py:122
  195.9 0.7 gather_fusion.1
  196.6 2.9 stack.2
  199.4 6.9 %all-to-all-start.2 = ((bf16[8,24,16,896]{3,2,1,0:T(8,128)(2,1)}), bf16[8,24,16,896]{3,2,1,0:T(8,128)(2,1)}, u32[]{:S(2)}, u32[]{:S(2)}) async-start(bf16[8,24,16,896]{3,2,1,0:T(8,128)(2,1)} %stack.2), calls=%async_computation.2 | async-start | bytes 11010048 | tf_op jit(solution)/shard_map/all_to_all | solution.py:129
  206.3 1.3 copy.117
  207.6 1.7 fusion.50
  209.4 0.6 copy-done.1
  210.0 0.6 fusion.40
  210.6 0.6 convolution_add_fusion.3
  211.1 1.7 fusion.42
  212.8 1.7 convolution_add_fusion.2
  214.5 1.7 fusion.44
  216.2 1.7 convolution_add_fusion.1
  217.9 1.7 fusion.27
  219.6 1.7 reshape.251
  221.4 0.8 multiply_reduce_fusion.1
  222.2 0.1 copy.108
  222.4 0.4 fusion.28
  222.9 108.4 %all-to-all-done.2 = bf16[8,24,16,896]{3,2,1,0:T(8,128)(2,1)} async-done(((bf16[8,24,16,896]{3,2,1,0:T(8,128)(2,1)}), bf16[8,24,16,896]{3,2,1,0:T(8,128)(2,1)}, u32[]{:S(2)}, u32[]{:S(2)}) %all-to-all-start.2) | async-done | bytes 5505056 | tf_op jit(solution)/shard_map/all_to_all | solution.py:129
  331.3 3.4 copy.107
  334.8 5.6 %multiply_reduce_fusion = (f32[3072,4]{0,1:T(4,128)S(1)}, f32[3072,4,128]{2,0,1:T(8,128)}) fusion(bf16[3072,896,1]{1,0,2:T(8,128)(2,1)S(1)} %bitcast.60, bf16[4,128,896]{2,1,0:T(8,128)(2,1)S(1)} %bitcast.68), kind=kOutput, calls=%fused_computation.9 | convolution fusion | flops 2821705728 | bytes 12763136 | tf_op jit(solution)/shard_map/dot_general | solution.py:132
  340.4 4.8 %convolution_convert_fusion = bf16[3072,512]{1,0:T(8,128)(2,1)} fusion(bf16[3072,896]{1,0:T(8,128)(2,1)S(1)} %bitcast.61, bf16[896,512]{1,0:T(8,128)(2,1)S(1)} %copy-done), kind=kOutput, calls=%fused_computation.11 | convolution fusion | flops 2820145152 | bytes 9568256 | tf_op jit(solution)/shard_map/dot_general | solution.py:133
  345.2 5.5 %reshape_reshape.7 = bf16[12,256,4,128]{3,2,1,0:T(4,128)(2,1)} reshape(bf16[3072,512]{1,0:T(8,128)(2,1)} %convolution_convert_fusion) | data formatting | bytes 6291456 | tf_op jit(solution)/shard_map/reshape;reshape | solution.py:26
  350.7 4.4 %multiply_convert_fusion = bf16[3072,4,128]{2,0,1:T(8,128)(2,1)S(1)} fusion(f32[3072,4,128]{2,0,1:T(8,128)} %get-tuple-element.12, f32[3072,4]{0,1:T(4,128)S(1)} %add_rsqrt_fusion), kind=kLoop, calls=%fused_computation.8 | loop fusion | flops 3145728 | bytes 9486336 | tf_op jit(solution)/shard_map/convert_element_type | solution.py:18
  355.2 1.3 fusion.16
  356.5 0.6 copy-done.2
  357.1 1.2 fusion.32
  358.3 0.6 copy.114
  358.9 0.1 copy.148
  359.1 1.1 concatenate.7
  (50 shorter events, 0.5 us)
Async XLA Ops:
  6.5 333.9 %copy-start = (bf16[896,512]{1,0:T(8,128)(2,1)S(1)}, bf16[896,512]{1,0:T(8,128)(2,1)}, u32[]{:S(2)}) copy-start(bf16[896,512]{1,0:T(8,128)(2,1)} %param.15) | copy-start | bytes 2752516
  6.5 58.9 %copy-start.12 = (s32[12,2]{0,1:T(2,128)S(1)}, s32[12,2]{0,1:T(2,128)}, u32[]{:S(2)}) copy-start(s32[12,2]{0,1:T(2,128)} %param.9) | copy-start | bytes 292
  6.5 118.7 %all-gather.9.cloned.1.call-start = ((), (), s32[]{:S(2)}) async-start(), calls=%async_computation.3 | async-start | bytes 7569408 | tf_op jit(solution)/shard_map/all_gather | solution.py:94
  31.9 123.9 %all-gather.11.cloned.1.call-start = ((), (), s32[]{:S(2)}) async-start(), calls=%async_computation.4 | async-start | bytes 6623232 | tf_op jit(solution)/shard_map/all_gather | solution.py:95
  53.5 11.9 %collective-permute-start = (bf16[705,512]{1,0:T(8,128)(2,1)S(1)}, bf16[705,512]{1,0:T(8,128)(2,1)S(1)}, u32[]{:S(2)}, u32[]{:S(2)}) collective-permute-start(bf16[705,512]{1,0:T(8,128)(2,1)S(1)} %slice.6), channel_id=1, source_target_pairs={{0,1},{1,2},{2,3},{3,4},{4,5},{5,6},{6,7},{7,0},{8,9},{9,10},{10,1... | collective-permute-start | bytes 2165768 | tf_op jit(solution)/shard_map/ppermute | solution.py:45
  54.2 40.7 %collective-permute-start.1 = (bf16[705,512]{1,0:T(8,128)(2,1)S(1)}, bf16[705,512]{1,0:T(8,128)(2,1)S(1)}, u32[]{:S(2)}, u32[]{:S(2)}) collective-permute-start(bf16[705,512]{1,0:T(8,128)(2,1)S(1)} %slice.6), channel_id=1, source_target_pairs={{0,7},{1,0},{2,1},{3,2},{4,3},{5,4},{6,5},{7,6},{8,15},{9,8},{10,9... | collective-permute-start | bytes 2165768 | tf_op jit(solution)/shard_map/ppermute | solution.py:48
  65.4 35.6 %copy-start.7 = (bf16[705,512]{1,0:T(8,128)(2,1)}, bf16[705,512]{1,0:T(8,128)(2,1)S(1)}, u32[]{:S(2)}) copy-start(bf16[705,512]{1,0:T(8,128)(2,1)S(1)} %collective-permute-done) | copy-start | bytes 2165764
  65.4 32.6 %collective-permute-start.2 = (bf16[705,512]{1,0:T(8,128)(2,1)S(1)}, bf16[705,512]{1,0:T(8,128)(2,1)}, u32[]{:S(2)}, u32[]{:S(2)}) collective-permute-start(bf16[705,512]{1,0:T(8,128)(2,1)S(1)} %collective-permute-done), channel_id=1, source_target_pairs={{0,1},{1,2},{2,3},{3,4},{4,5},{5,6},{6,7},{7,0},{8,9},{9,10},{10,1... | collective-permute-start | bytes 2165768 | tf_op jit(solution)/shard_map/ppermute | solution.py:45
  66.7 34.0 %all-to-all-start = ((s32[32,1,2]{2,1,0:T(1,128)}), s32[32,1,2]{2,1,0:T(1,128)S(1)}, u32[]{:S(2)}, u32[]{:S(2)}) async-start(s32[32,1,2]{2,1,0:T(1,128)} %bitcast.11), calls=%async_computation | async-start | bytes 32768 | tf_op jit(solution)/shard_map/all_to_all | solution.py:120
  95.0 6.1 %copy-start.9 = (bf16[705,512]{1,0:T(8,128)(2,1)}, bf16[705,512]{1,0:T(8,128)(2,1)S(1)}, u32[]{:S(2)}) copy-start(bf16[705,512]{1,0:T(8,128)(2,1)S(1)} %collective-permute-done.1) | copy-start | bytes 2165764
  95.0 18.5 %collective-permute-start.3 = (bf16[705,512]{1,0:T(8,128)(2,1)S(1)}, bf16[705,512]{1,0:T(8,128)(2,1)}, u32[]{:S(2)}, u32[]{:S(2)}) collective-permute-start(bf16[705,512]{1,0:T(8,128)(2,1)S(1)} %collective-permute-done.1), channel_id=1, source_target_pairs={{0,7},{1,0},{2,1},{3,2},{4,3},{5,4},{6,5},{7,6},{8,15},{9,8},{10,9... | collective-permute-start | bytes 2165768 | tf_op jit(solution)/shard_map/ppermute | solution.py:48
  98.0 27.3 %collective-permute-start.4 = (bf16[705,512]{1,0:T(8,128)(2,1)}, bf16[705,512]{1,0:T(8,128)(2,1)}, u32[]{:S(2)}, u32[]{:S(2)}) collective-permute-start(bf16[705,512]{1,0:T(8,128)(2,1)} %collective-permute-done.2), channel_id=1, source_target_pairs={{0,1},{1,2},{2,3},{3,4},{4,5},{5,6},{6,7},{7,0},{8,9},{9,10},{10,1... | collective-permute-start | bytes 2165768 | tf_op jit(solution)/shard_map/ppermute | solution.py:45
  121.7 43.9 %collective-permute-start.5 = (bf16[705,512]{1,0:T(8,128)(2,1)}, bf16[705,512]{1,0:T(8,128)(2,1)}, u32[]{:S(2)}, u32[]{:S(2)}) collective-permute-start(bf16[705,512]{1,0:T(8,128)(2,1)} %collective-permute-done.3), channel_id=1, source_target_pairs={{0,7},{1,0},{2,1},{3,2},{4,3},{5,4},{6,5},{7,6},{8,15},{9,8},{10,9... | collective-permute-start | bytes 2165768 | tf_op jit(solution)/shard_map/ppermute | solution.py:48
  125.3 40.4 %collective-permute-start.6 = (bf16[705,512]{1,0:T(8,128)(2,1)}, bf16[705,512]{1,0:T(8,128)(2,1)S(1)}, u32[]{:S(2)}, u32[]{:S(2)}) collective-permute-start(bf16[705,512]{1,0:T(8,128)(2,1)} %collective-permute-done.4), channel_id=1, source_target_pairs={{0,1},{1,2},{2,3},{3,4},{4,5},{5,6},{6,7},{7,0},{8,9},{9,10},{10,1... | collective-permute-start | bytes 2165768 | tf_op jit(solution)/shard_map/ppermute | solution.py:45
  165.7 30.2 %copy-start.5 = (bf16[705,512]{1,0:T(8,128)(2,1)}, bf16[705,512]{1,0:T(8,128)(2,1)S(1)}, u32[]{:S(2)}) copy-start(bf16[705,512]{1,0:T(8,128)(2,1)S(1)} %collective-permute-done.6) | copy-start | bytes 2165764
  165.7 30.2 %all-to-all-start.1 = ((bf16[32,2,16,896]{3,2,1,0:T(8,128)(2,1)}), bf16[32,2,16,896]{3,2,1,0:T(8,128)(2,1)S(1)}, u32[]{:S(2)}, u32[]{:S(2)}) async-start(bf16[32,2,16,896]{3,2,1,0:T(8,128)(2,1)} %bitcast.13), calls=%async_computation.1 | async-start | bytes 3670016 | tf_op jit(solution)/shard_map/all_to_all | solution.py:122
  199.4 6.9 %copy-start.3 = (bf16[896,512]{1,0:T(8,128)(2,1)S(1)}, bf16[896,512]{1,0:T(8,128)(2,1)}, u32[]{:S(2)}) copy-start(bf16[896,512]{1,0:T(8,128)(2,1)} %param.14) | copy-start | bytes 2752516
  199.4 8.2 %copy-start.11 = (bf16[768,512]{1,0:T(8,128)(2,1)S(1)}, bf16[768,512]{1,0:T(8,128)(2,1)}, u32[]{:S(2)}) copy-start(bf16[768,512]{1,0:T(8,128)(2,1)} %param.8) | copy-start | bytes 2359300
  199.4 131.9 %all-to-all-start.2 = ((bf16[8,24,16,896]{3,2,1,0:T(8,128)(2,1)}), bf16[8,24,16,896]{3,2,1,0:T(8,128)(2,1)}, u32[]{:S(2)}, u32[]{:S(2)}) async-start(bf16[8,24,16,896]{3,2,1,0:T(8,128)(2,1)} %stack.2), calls=%async_computation.2 | async-start | bytes 11010048 | tf_op jit(solution)/shard_map/all_to_all | solution.py:129
  206.3 3.1 copy-start.8
  207.6 2.3 copy-start.1
  207.6 2.9 copy-start.10
  214.5 3.4 copy-start.6
  331.3 3.4 copy-start.4
  355.2 1.9 copy-start.2
Sparse Core Ops, SparseCore 0:
  32.0 66.9 all-gather.8
  101.6 54.1 all-gather.10
